TPU v7x, 128 devices: a whole 4x4x4 slice. The times are simulated.
128 devices in a mesh: seg: 8 (over x, core), leaf: 16 (over z, y).
Axes of the slice: x: 4, y: 4, z: 4, core: 2. Of those that a mesh axis runs over, the one named last changes fastest.
Arguments:
- queries: bfloat16 [32, 512, 5120], P('seg', 'leaf'), may hold values from -160 to 160
- leaf_keys: bfloat16 [32, 512, 1024], P('seg', 'leaf'), may hold values from -5 to 5
- leaf_values: bfloat16 [32, 512, 1024], P('seg', 'leaf'), may hold values from -6 to 6
- inner_keys: bfloat16 [16, 512, 1024], P('seg', 'leaf'), may hold values from -6 to 6
- inner_values: bfloat16 [16, 512, 1024], P('seg', 'leaf'), may hold values from -6 to 6
- out_grad: bfloat16 [32, 512, 5120], P('seg', 'leaf'), may hold values from -6 to 6
- ancestors: int32 [32, 4], replicated, may hold values from 0 to 15, as said below
- depths: int32 [32], replicated, may hold values from 3 to 4, as said below
Outputs:
- attention: bfloat16 [32, 512, 5120], P('seg', 'leaf')
- query_grad: bfloat16 [32, 512, 5120], P('seg', 'leaf')
- leaf_key_grad: bfloat16 [32, 512, 1024], P('seg', 'leaf')
- leaf_value_grad: bfloat16 [32, 512, 1024], P('seg', 'leaf')
- inner_key_grad: bfloat16 [16, 512, 1024], P('seg', 'leaf')
- inner_value_grad: bfloat16 [16, 512, 1024], P('seg', 'leaf')
Inputs may be any that keep to these rules, and one draw needn't show every extreme that they name: `ancestors`: leaves l and m with l // 4 == m // 4 have the same row. Entry k of a row is the leaf's ancestor at tree level k, entry 0 the prompt's segment; entries at or past the leaf's depth are 0. The live entries of one row have different values of i // 2. `depths`: equal within each aligned block of 4 leaves; some leaf has 4.
All inputs are finite; a program needn't handle non-finite values.
Results may differ from a plain program's by a relative error of at most 0.03.
Values may be sent and summed in bfloat16 or wider, within the bound.
No kernel may reach another device: no remote copies, remote signals or barrier semaphores. Data moves between devices by JAX's collectives and lax.ppermute only.
A program may use at most 128 MiB of HBM per device.

v0:
```python
import math
import jax
import jax.numpy as jnp
from jax import lax
from jax.sharding import PartitionSpec as P

HD = 128
NEG_FILL = -1e30


def head_major(packed, kv_heads, head_size):
    block_count, rows_here = (packed.shape[0], packed.shape[1])
    shaped = packed.reshape(block_count, rows_here, 2, kv_heads, head_size)
    return shaped.transpose(3, 0, 1, 2, 4).reshape(kv_heads, block_count, rows_here, 2 * head_size)


def column_major(stacked, kv_heads, head_size):
    block_count, rows_here = (stacked.shape[1], stacked.shape[2])
    shaped = stacked.reshape(kv_heads, block_count, rows_here, 2, head_size)
    return shaped.transpose(1, 2, 3, 0, 4).reshape(block_count, rows_here, 2 * kv_heads * head_size)


def attend_block(
    query_row_set,
    gradient_row_set,
    key_anc,
    value_anc,
    private_keys,
    private_values,
    anc_visible,
    own_visible,
):
    logit_scale = 1.0 / math.sqrt(query_row_set.shape[-1])
    score_anc = (
        jnp.einsum("bmd,ad->bma", query_row_set, key_anc, preferred_element_type=jnp.float32)
        * logit_scale
    )
    score_own = (
        jnp.einsum("flh,feh->fle", query_row_set, private_keys, preferred_element_type=jnp.float32)
        * logit_scale
    )
    score_anc = jnp.where(anc_visible[None, None, :], score_anc, NEG_FILL)
    score_own = jnp.where(own_visible[None], score_own, NEG_FILL)
    highest = jnp.maximum(
        jnp.max(score_anc, axis=-1, keepdims=True), jnp.max(score_own, axis=-1, keepdims=True)
    )
    weight_anc = jnp.exp(score_anc - highest)
    weight_own = jnp.exp(score_own - highest)
    denom_sum = jnp.sum(weight_anc, axis=-1, keepdims=True) + jnp.sum(
        weight_own, axis=-1, keepdims=True
    )
    prob_anc = weight_anc / denom_sum
    prob_own = weight_own / denom_sum
    round_anc = prob_anc.astype(jnp.bfloat16)
    private_round = prob_own.astype(jnp.bfloat16)
    attention_result = jnp.einsum(
        "bma,ad->bmd", round_anc, value_anc, preferred_element_type=jnp.float32
    ) + jnp.einsum(
        "oiz,ozv->oiv", private_round, private_values, preferred_element_type=jnp.float32
    )
    result_round = attention_result.astype(jnp.bfloat16)
    delta_rows = jnp.sum(
        gradient_row_set.astype(jnp.float32) * result_round.astype(jnp.float32),
        axis=-1,
        keepdims=True,
    )
    dprob_anc = jnp.einsum(
        "bmd,ad->bma", gradient_row_set, value_anc, preferred_element_type=jnp.float32
    )
    own_probability_grad = jnp.einsum(
        "flh,feh->fle", gradient_row_set, private_values, preferred_element_type=jnp.float32
    )
    dscore_anc = (prob_anc * (dprob_anc - delta_rows)).astype(jnp.bfloat16)
    own_score_grad = (prob_own * (own_probability_grad - delta_rows)).astype(jnp.bfloat16)
    query_portion = (
        jnp.einsum("bma,ad->bmd", dscore_anc, key_anc, preferred_element_type=jnp.float32)
        + jnp.einsum(
            "oiz,ozv->oiv", own_score_grad, private_keys, preferred_element_type=jnp.float32
        )
    ) * logit_scale
    dkey_anc = (
        jnp.einsum("bma,bmd->ad", dscore_anc, query_row_set, preferred_element_type=jnp.float32)
        * logit_scale
    )
    dvalue_anc = jnp.einsum(
        "bma,bmd->ad", round_anc, gradient_row_set, preferred_element_type=jnp.float32
    )
    dkey_own = (
        jnp.einsum(
            "ers,erc->esc", own_score_grad, query_row_set, preferred_element_type=jnp.float32
        )
        * logit_scale
    )
    dvalue_own = jnp.einsum(
        "ers,erc->esc", private_round, gradient_row_set, preferred_element_type=jnp.float32
    )
    return (result_round, query_portion, dkey_anc, dvalue_anc, dkey_own, dvalue_own)


def on_device(
    queries, leaf_keys, leaf_values, inner_keys, inner_values, out_grad, ancestors, depths
):
    seg_count = lax.axis_size("seg")
    leaf_count = lax.axis_size("leaf")
    seg_here = lax.axis_index("seg")
    leaf_here = lax.axis_index("leaf")
    leaf_dev, rows_here, query_width = queries.shape
    slot_count = inner_keys.shape[0]
    key_width = leaf_keys.shape[2]
    kv_heads = key_width // HD
    group_heads = query_width // key_width
    seg_len = rows_here * leaf_count
    levels = ancestors.shape[1]
    group_lists = ancestors[::leaf_dev]
    group_depth = depths[::leaf_dev]
    owners = group_lists // slot_count
    slot_of = group_lists % slot_count
    level_ids = jnp.arange(levels, dtype=jnp.int32)
    alive_levels = level_ids[None, :] < group_depth[:, None]
    served = alive_levels & (owners == seg_here)
    slot_ids = jnp.arange(slot_count, dtype=jnp.int32)
    serve_pick = jnp.sum(
        (served[:, :, None] & (slot_of[:, :, None] == slot_ids[None, None, :])).astype(jnp.float32),
        axis=1,
    ).astype(jnp.bfloat16)
    stored = jnp.concatenate([inner_keys, inner_values], axis=2)
    outgoing = jnp.einsum(
        "gs,src->grc", serve_pick, stored, preferred_element_type=jnp.float32
    ).astype(jnp.bfloat16)
    arrived = lax.all_to_all(outgoing, "seg", split_axis=0, concat_axis=0, tiled=True)
    my_owners = jnp.take(owners, seg_here, axis=0)
    my_alive = jnp.take(alive_levels, seg_here, axis=0)
    ancestor_rows = jnp.where(
        my_alive[:, None, None], jnp.take(arrived, my_owners, axis=0), jnp.zeros((), jnp.bfloat16)
    )
    own_rows = jnp.concatenate([leaf_keys, leaf_values], axis=2)
    anc_visible = jnp.repeat(my_alive, seg_len)
    blocks = jnp.concatenate([ancestor_rows, own_rows], axis=0)
    by_head = head_major(blocks, kv_heads, HD)
    query_heads = queries.reshape(leaf_dev, rows_here, kv_heads, group_heads * HD).transpose(
        2, 0, 1, 3
    )
    grad_heads = out_grad.reshape(leaf_dev, rows_here, kv_heads, group_heads * HD).transpose(
        2, 0, 1, 3
    )
    row_ids = leaf_here * rows_here + jnp.arange(rows_here, dtype=jnp.int32)
    causal = jnp.arange(seg_len, dtype=jnp.int32)[None, :] <= row_ids[:, None]
    own_visible = jnp.repeat(causal, group_heads, axis=0)

    def head_step(operands):
        query_head, grad_head, packed_head = operands
        whole_rows = lax.all_gather(packed_head, "leaf", axis=1, tiled=True)
        key_anc = whole_rows[:levels, :, :HD].reshape(levels * seg_len, HD)
        value_anc = whole_rows[:levels, :, HD:].reshape(levels * seg_len, HD)
        private_keys = whole_rows[levels:, :, :HD]
        private_values = whole_rows[levels:, :, HD:]
        query_row_set = query_head.reshape(leaf_dev, rows_here * group_heads, HD)
        gradient_row_set = grad_head.reshape(leaf_dev, rows_here * group_heads, HD)
        result_round, query_portion, dkey_anc, dvalue_anc, dkey_own, dvalue_own = attend_block(
            query_row_set,
            gradient_row_set,
            key_anc,
            value_anc,
            private_keys,
            private_values,
            anc_visible,
            own_visible,
        )
        key_grads = jnp.concatenate([dkey_anc.reshape(levels, seg_len, HD), dkey_own], axis=0)
        value_grads = jnp.concatenate([dvalue_anc.reshape(levels, seg_len, HD), dvalue_own], axis=0)
        reduced = lax.psum_scatter(
            jnp.concatenate([key_grads, value_grads], axis=2),
            "leaf",
            scatter_dimension=1,
            tiled=True,
        )
        return (
            result_round.reshape(leaf_dev, rows_here, group_heads * HD),
            query_portion.astype(jnp.bfloat16).reshape(leaf_dev, rows_here, group_heads * HD),
            reduced,
        )

    result_heads, dquery_heads, reduced_heads = lax.map(
        head_step, (query_heads, grad_heads, by_head)
    )
    attention = result_heads.transpose(1, 2, 0, 3).reshape(leaf_dev, rows_here, query_width)
    query_grad = dquery_heads.transpose(1, 2, 0, 3).reshape(leaf_dev, rows_here, query_width)
    summed = column_major(reduced_heads, kv_heads, HD)
    anc_part = summed[:levels]
    own_grads = summed[levels:].astype(jnp.bfloat16)
    leaf_key_grad = own_grads[:, :, :key_width]
    leaf_value_grad = own_grads[:, :, key_width:]
    part_round = anc_part.astype(jnp.bfloat16)
    seg_ids = jnp.arange(seg_count, dtype=jnp.int32)
    homeward_pick = ((my_owners[None, :] == seg_ids[:, None]) & my_alive[None, :]).astype(
        jnp.bfloat16
    )
    homeward = jnp.einsum(
        "ok,krc->orc", homeward_pick, part_round, preferred_element_type=jnp.float32
    ).astype(jnp.bfloat16)
    returned = lax.all_to_all(homeward, "seg", split_axis=0, concat_axis=0, tiled=True)
    collected = jnp.einsum(
        "gs,grc->src", serve_pick, returned, preferred_element_type=jnp.float32
    ).astype(jnp.bfloat16)
    return (
        attention,
        query_grad,
        leaf_key_grad,
        leaf_value_grad,
        collected[:, :, :key_width],
        collected[:, :, key_width:],
    )


def solution(mesh):
    return jax.shard_map(
        on_device,
        mesh=mesh,
        in_specs=(
            P("seg", "leaf", None),
            P("seg", "leaf", None),
            P("seg", "leaf", None),
            P("seg", "leaf", None),
            P("seg", "leaf", None),
            P("seg", "leaf", None),
            P(),
            P(),
        ),
        out_specs=(
            P("seg", "leaf", None),
            P("seg", "leaf", None),
            P("seg", "leaf", None),
            P("seg", "leaf", None),
            P("seg", "leaf", None),
            P("seg", "leaf", None),
        ),
        check_vma=False,
    )
```

profile of v0, /device:TPU:1, one launch (start us, length us, event | category | flops | bytes accessed | tf_op | source)
XLA Modules:
  0.0 1323.1 jit_solution(9653723527980471428)
XLA Ops:
  13.4 5.8 all-to-all-start
  25.5 8.7 all-to-all-done
  39.1 1248.2 %while.17 = (s32[]{:T(128)}, bf16[8,4,32,640]{3,2,1,0:T(8,128)(2,1)}, bf16[8,4,32,640]{3,2,1,0:T(8,128)(2,1)}, bf16[8,8,32,256]{3,1,2,0:T(8,128)(2,1)}, bf16[8,4...) while((s32[]{:T(128)}, ...), condition=%wide.region_8.9_spmd.clone, body=%wide.region_1.8_spmd.clone.sunk | while | flops 2550151168 | bytes 133755288 | solution.py:183
  43.9 43.0 %all-gather.6.cloned.1.call-done = bf16[1,8,512,256]{3,2,1,0:T(8,128)(2,1)} async-done(((bf16[1,8,32,256]{3,2,1,0:T(8,128)(2,1)}), bf16[1,8,512,256]{3,2,1,0:T(8,128)(2,1)}) %all-gather.6.cloned.1.call-update) | async-done | bytes 2097168 | tf_op jit(solution)/shard_map/while/body/eval_jaxpr/all_gather | solution.py:152
  110.3 5.5 copy.107
  120.9 72.7 %reduce-scatter.2.cloned.1.call-done = f32[8,32,256]{2,0,1:T(8,128)} async-done(((f32[8,512,256]{2,0,1:T(8,128)}), f32[8,32,256]{2,0,1:T(8,128)}) %reduce-scatter.2.cloned.1.call-update) | async-done | bytes 262160 | tf_op jit(solution)/shard_map/while/body/eval_jaxpr/reduce_scatter | solution.py:171
  200.0 43.1 %all-gather.6.cloned.1.call-done = bf16[1,8,512,256]{3,2,1,0:T(8,128)(2,1)} async-done(((bf16[1,8,32,256]{3,2,1,0:T(8,128)(2,1)}), bf16[1,8,512,256]{3,2,1,0:T(8,128)(2,1)}) %all-gather.6.cloned.1.call-update) | async-done | bytes 2097168 | tf_op jit(solution)/shard_map/while/body/eval_jaxpr/all_gather | solution.py:152
  266.4 5.5 copy.107
  277.0 72.7 %reduce-scatter.2.cloned.1.call-done = f32[8,32,256]{2,0,1:T(8,128)} async-done(((f32[8,512,256]{2,0,1:T(8,128)}), f32[8,32,256]{2,0,1:T(8,128)}) %reduce-scatter.2.cloned.1.call-update) | async-done | bytes 262160 | tf_op jit(solution)/shard_map/while/body/eval_jaxpr/reduce_scatter | solution.py:171
  356.1 42.8 %all-gather.6.cloned.1.call-done = bf16[1,8,512,256]{3,2,1,0:T(8,128)(2,1)} async-done(((bf16[1,8,32,256]{3,2,1,0:T(8,128)(2,1)}), bf16[1,8,512,256]{3,2,1,0:T(8,128)(2,1)}) %all-gather.6.cloned.1.call-update) | async-done | bytes 2097168 | tf_op jit(solution)/shard_map/while/body/eval_jaxpr/all_gather | solution.py:152
  422.2 5.5 copy.107
  432.8 72.6 %reduce-scatter.2.cloned.1.call-done = f32[8,32,256]{2,0,1:T(8,128)} async-done(((f32[8,512,256]{2,0,1:T(8,128)}), f32[8,32,256]{2,0,1:T(8,128)}) %reduce-scatter.2.cloned.1.call-update) | async-done | bytes 262160 | tf_op jit(solution)/shard_map/while/body/eval_jaxpr/reduce_scatter | solution.py:171
  511.8 43.1 %all-gather.6.cloned.1.call-done = bf16[1,8,512,256]{3,2,1,0:T(8,128)(2,1)} async-done(((bf16[1,8,32,256]{3,2,1,0:T(8,128)(2,1)}), bf16[1,8,512,256]{3,2,1,0:T(8,128)(2,1)}) %all-gather.6.cloned.1.call-update) | async-done | bytes 2097168 | tf_op jit(solution)/shard_map/while/body/eval_jaxpr/all_gather | solution.py:152
  588.8 72.7 %reduce-scatter.2.cloned.1.call-done = f32[8,32,256]{2,0,1:T(8,128)} async-done(((f32[8,512,256]{2,0,1:T(8,128)}), f32[8,32,256]{2,0,1:T(8,128)}) %reduce-scatter.2.cloned.1.call-update) | async-done | bytes 262160 | tf_op jit(solution)/shard_map/while/body/eval_jaxpr/reduce_scatter | solution.py:171
  668.0 43.1 %all-gather.6.cloned.1.call-done = bf16[1,8,512,256]{3,2,1,0:T(8,128)(2,1)} async-done(((bf16[1,8,32,256]{3,2,1,0:T(8,128)(2,1)}), bf16[1,8,512,256]{3,2,1,0:T(8,128)(2,1)}) %all-gather.6.cloned.1.call-update) | async-done | bytes 2097168 | tf_op jit(solution)/shard_map/while/body/eval_jaxpr/all_gather | solution.py:152
  745.0 72.7 %reduce-scatter.2.cloned.1.call-done = f32[8,32,256]{2,0,1:T(8,128)} async-done(((f32[8,512,256]{2,0,1:T(8,128)}), f32[8,32,256]{2,0,1:T(8,128)}) %reduce-scatter.2.cloned.1.call-update) | async-done | bytes 262160 | tf_op jit(solution)/shard_map/while/body/eval_jaxpr/reduce_scatter | solution.py:171
  824.1 43.1 %all-gather.6.cloned.1.call-done = bf16[1,8,512,256]{3,2,1,0:T(8,128)(2,1)} async-done(((bf16[1,8,32,256]{3,2,1,0:T(8,128)(2,1)}), bf16[1,8,512,256]{3,2,1,0:T(8,128)(2,1)}) %all-gather.6.cloned.1.call-update) | async-done | bytes 2097168 | tf_op jit(solution)/shard_map/while/body/eval_jaxpr/all_gather | solution.py:152
  901.1 72.7 %reduce-scatter.2.cloned.1.call-done = f32[8,32,256]{2,0,1:T(8,128)} async-done(((f32[8,512,256]{2,0,1:T(8,128)}), f32[8,32,256]{2,0,1:T(8,128)}) %reduce-scatter.2.cloned.1.call-update) | async-done | bytes 262160 | tf_op jit(solution)/shard_map/while/body/eval_jaxpr/reduce_scatter | solution.py:171
  980.2 43.1 %all-gather.6.cloned.1.call-done = bf16[1,8,512,256]{3,2,1,0:T(8,128)(2,1)} async-done(((bf16[1,8,32,256]{3,2,1,0:T(8,128)(2,1)}), bf16[1,8,512,256]{3,2,1,0:T(8,128)(2,1)}) %all-gather.6.cloned.1.call-update) | async-done | bytes 2097168 | tf_op jit(solution)/shard_map/while/body/eval_jaxpr/all_gather | solution.py:152
  1057.2 72.6 %reduce-scatter.2.cloned.1.call-done = f32[8,32,256]{2,0,1:T(8,128)} async-done(((f32[8,512,256]{2,0,1:T(8,128)}), f32[8,32,256]{2,0,1:T(8,128)}) %reduce-scatter.2.cloned.1.call-update) | async-done | bytes 262160 | tf_op jit(solution)/shard_map/while/body/eval_jaxpr/reduce_scatter | solution.py:171
  1136.3 42.8 %all-gather.6.cloned.1.call-done = bf16[1,8,512,256]{3,2,1,0:T(8,128)(2,1)} async-done(((bf16[1,8,32,256]{3,2,1,0:T(8,128)(2,1)}), bf16[1,8,512,256]{3,2,1,0:T(8,128)(2,1)}) %all-gather.6.cloned.1.call-update) | async-done | bytes 2097168 | tf_op jit(solution)/shard_map/while/body/eval_jaxpr/all_gather | solution.py:152
  1213.0 72.7 %reduce-scatter.2.cloned.1.call-done = f32[8,32,256]{2,0,1:T(8,128)} async-done(((f32[8,512,256]{2,0,1:T(8,128)}), f32[8,32,256]{2,0,1:T(8,128)}) %reduce-scatter.2.cloned.1.call-update) | async-done | bytes 262160 | tf_op jit(solution)/shard_map/while/body/eval_jaxpr/reduce_scatter | solution.py:171
  1292.5 6.7 all-to-all-start.1
  1303.6 10.6 all-to-all-done.1
  (499 shorter events, 333.9 us)
Async XLA Ops:
  11.8 7.4 copy-start.8
  13.4 20.9 %all-to-all-start = ((bf16[8,32,2048]{2,1,0:T(8,128)(2,1)}), bf16[8,32,2048]{2,1,0:T(8,128)(2,1)}, u32[]{:S(2)}, u32[]{:S(2)}) async-start(bf16[8,32,2048]{2,1,0:T(8,128)(2,1)} %copy.66), calls=%async_computation.1 | async-start | bytes 2097152 | tf_op jit(solution)/shard_map/all_to_all | solution.py:130
  25.0 11.3 copy-start.7
  25.2 11.2 copy-start.14
  39.1 47.9 %all-gather.6.cloned.1.call-start = ((), (), s32[]{:S(2)}) async-start(), calls=%async_computation.3 | async-start | bytes 2228224 | tf_op jit(solution)/shard_map/while/body/eval_jaxpr/all_gather | solution.py:152
  40.7 152.9 %reduce-scatter.2.cloned.1.call-start = ((), (), s32[]{:S(2)}) async-start(), calls=%async_computation.4 | async-start | bytes 4456448 | tf_op jit(solution)/shard_map/while/body/eval_jaxpr/reduce_scatter | solution.py:171
  115.8 4.2 copy-start.5
  195.2 47.9 %all-gather.6.cloned.1.call-start = ((), (), s32[]{:S(2)}) async-start(), calls=%async_computation.3 | async-start | bytes 2228224 | tf_op jit(solution)/shard_map/while/body/eval_jaxpr/all_gather | solution.py:152
  196.7 152.9 %reduce-scatter.2.cloned.1.call-start = ((), (), s32[]{:S(2)}) async-start(), calls=%async_computation.4 | async-start | bytes 4456448 | tf_op jit(solution)/shard_map/while/body/eval_jaxpr/reduce_scatter | solution.py:171
  271.9 4.2 copy-start.5
  351.3 47.6 %all-gather.6.cloned.1.call-start = ((), (), s32[]{:S(2)}) async-start(), calls=%async_computation.3 | async-start | bytes 2228224 | tf_op jit(solution)/shard_map/while/body/eval_jaxpr/all_gather | solution.py:152
  352.9 152.5 %reduce-scatter.2.cloned.1.call-start = ((), (), s32[]{:S(2)}) async-start(), calls=%async_computation.4 | async-start | bytes 4456448 | tf_op jit(solution)/shard_map/while/body/eval_jaxpr/reduce_scatter | solution.py:171
  507.0 47.9 %all-gather.6.cloned.1.call-start = ((), (), s32[]{:S(2)}) async-start(), calls=%async_computation.3 | async-start | bytes 2228224 | tf_op jit(solution)/shard_map/while/body/eval_jaxpr/all_gather | solution.py:152
  508.6 152.9 %reduce-scatter.2.cloned.1.call-start = ((), (), s32[]{:S(2)}) async-start(), calls=%async_computation.4 | async-start | bytes 4456448 | tf_op jit(solution)/shard_map/while/body/eval_jaxpr/reduce_scatter | solution.py:171
  663.1 47.9 %all-gather.6.cloned.1.call-start = ((), (), s32[]{:S(2)}) async-start(), calls=%async_computation.3 | async-start | bytes 2228224 | tf_op jit(solution)/shard_map/while/body/eval_jaxpr/all_gather | solution.py:152
  664.7 152.9 %reduce-scatter.2.cloned.1.call-start = ((), (), s32[]{:S(2)}) async-start(), calls=%async_computation.4 | async-start | bytes 4456448 | tf_op jit(solution)/shard_map/while/body/eval_jaxpr/reduce_scatter | solution.py:171
  819.3 47.9 %all-gather.6.cloned.1.call-start = ((), (), s32[]{:S(2)}) async-start(), calls=%async_computation.3 | async-start | bytes 2228224 | tf_op jit(solution)/shard_map/while/body/eval_jaxpr/all_gather | solution.py:152
  820.9 152.9 %reduce-scatter.2.cloned.1.call-start = ((), (), s32[]{:S(2)}) async-start(), calls=%async_computation.4 | async-start | bytes 4456448 | tf_op jit(solution)/shard_map/while/body/eval_jaxpr/reduce_scatter | solution.py:171
  975.4 47.9 %all-gather.6.cloned.1.call-start = ((), (), s32[]{:S(2)}) async-start(), calls=%async_computation.3 | async-start | bytes 2228224 | tf_op jit(solution)/shard_map/while/body/eval_jaxpr/all_gather | solution.py:152
  977.0 152.8 %reduce-scatter.2.cloned.1.call-start = ((), (), s32[]{:S(2)}) async-start(), calls=%async_computation.4 | async-start | bytes 4456448 | tf_op jit(solution)/shard_map/while/body/eval_jaxpr/reduce_scatter | solution.py:171
  1131.4 47.6 %all-gather.6.cloned.1.call-start = ((), (), s32[]{:S(2)}) async-start(), calls=%async_computation.3 | async-start | bytes 2228224 | tf_op jit(solution)/shard_map/while/body/eval_jaxpr/all_gather | solution.py:152
  1133.0 152.6 %reduce-scatter.2.cloned.1.call-start = ((), (), s32[]{:S(2)}) async-start(), calls=%async_computation.4 | async-start | bytes 4456448 | tf_op jit(solution)/shard_map/while/body/eval_jaxpr/reduce_scatter | solution.py:171
  1292.5 21.7 %all-to-all-start.1 = ((bf16[8,32,2048]{2,1,0:T(8,128)(2,1)}), bf16[8,32,2048]{2,1,0:T(8,128)(2,1)S(1)}, u32[]{:S(2)}, u32[]{:S(2)}) async-start(bf16[8,32,2048]{2,1,0:T(8,128)(2,1)} %copy.74), calls=%async_computation.2 | async-start | bytes 2097152 | tf_op jit(solution)/shard_map/all_to_all | solution.py:201
  1301.1 13.1 copy-start.17
  (61 other events, 149.0 us)
Sparse Core Ops, SparseCore 0:
  42.6 44.3 all-gather.5
  115.9 77.5 reduce-scatter.1
  198.7 44.3 all-gather.5
  272.0 77.5 reduce-scatter.1
  354.5 44.3 all-gather.5
  427.8 77.5 reduce-scatter.1
  510.5 44.3 all-gather.5
  583.9 77.6 reduce-scatter.1
  666.6 44.3 all-gather.5
  740.0 77.6 reduce-scatter.1
  822.8 44.3 all-gather.5
  896.1 77.6 reduce-scatter.1
  978.9 44.3 all-gather.5
  1052.2 77.5 reduce-scatter.1
  1134.7 44.3 all-gather.5
  1208.0 77.5 reduce-scatter.1
where the time goes:
time: 1330 us; the launch traced here: 1320 us
  waiting for transfers between devices  945 us (71%)
  local copies, waits for them, and re-layouts  172 us (13%)
  matrix products  130 us (10%)
  other arithmetic  47.1 us (4%)
  between operations  14 us (1%)
    reduce_scatter x8, waiting for transfers between devices, head_step(): lax.psum_scatter(jnp.concatenate([key_grads, value_grads], axis=2), 'leaf...  581 us
    all_gather x8, waiting for transfers between devices, head_step(): whole_rows = lax.all_gather(packed_head, 'leaf', axis=1, tiled=True)  344 us
    concatenate x8, local copies, waits for them, and re-layouts, head_step(): jnp.concatenate([key_grads, value_grads], axis=2)  43.7 us
    dynamic_slice x24, local copies, waits for them, and re-layouts, on_device(): lax.map(head_step, (query_heads, grad_heads, by_head))  27.5 us
  transfers between devices with their start and end apart: 18, of which 18 were waited for; matrix products, arithmetic and copies ran while one was open for 6% of the time, Pallas kernels for 0%

commit v1 on v0

--- a/solution.py
+++ b/solution.py
@@ -149,7 +149,26 @@
 
     def head_step(operands):
         query_head, grad_head, packed_head = operands
-        whole_rows = lax.all_gather(packed_head, "leaf", axis=1, tiled=True)
+        peers, index, rows = (lax.axis_size("leaf"), lax.axis_index("leaf"), packed_head.shape[1])
+        forward = [(i, (i + 1) % peers) for i in range(peers)]
+        backward = [(i, (i - 1) % peers) for i in range(peers)]
+        filled = jnp.zeros(
+            (*packed_head.shape[:1], peers * rows, *packed_head.shape[1 + 1 :]), packed_head.dtype
+        )
+        filled = lax.dynamic_update_slice_in_dim(filled, packed_head, index * rows, axis=1)
+        from_left = from_right = packed_head
+        half = peers // 2
+        for step in range(1, half + 1):
+            from_left = lax.ppermute(from_left, "leaf", forward)
+            filled = lax.dynamic_update_slice_in_dim(
+                filled, from_left, (index - step) % peers * rows, axis=1
+            )
+            if step < peers - half:
+                from_right = lax.ppermute(from_right, "leaf", backward)
+                filled = lax.dynamic_update_slice_in_dim(
+                    filled, from_right, (index + step) % peers * rows, axis=1
+                )
+        whole_rows = filled
         key_anc = whole_rows[:levels, :, :HD].reshape(levels * seg_len, HD)
         value_anc = whole_rows[:levels, :, HD:].reshape(levels * seg_len, HD)
         private_keys = whole_rows[levels:, :, :HD]

time: 1330 us -> 1470 us (1.11)
  starting transfers between devices: 12.9 us -> 290 us
  waiting for transfers between devices: 945 us -> 828 us
  local copies, waits for them, and re-layouts: 172 us -> 149 us
    all_gather x8 -> x0, waiting for transfers between devices: 344 us -> none  [head_step(): whole_rows = lax.all_gather(packed_head, 'leaf', axis=1, tiled=True)]
    ppermute x0 -> x120, starting transfers between devices: none -> 277 us  [the longest x56 271 us: head_step(): from_right = lax.ppermute(from_right, 'leaf', backward)]
    ppermute x0 -> x120, waiting for transfers between devices: none -> 178 us  [the longest x64 177 us: head_step(): from_left = lax.ppermute(from_left, 'leaf', forward)]
    reduce_scatter x8, waiting for transfers between devices: 581 us -> 631 us  [head_step(): lax.psum_scatter(jnp.concatenate([key_grads, value_grads], axis=2), 'leaf...]
    dot_general x8, matrix products: 4.97 us -> 20.1 us  [attend_block(): jnp.einsum('bma,bmd->ad', round_anc, gradient_row_set, preferred_element_...]
  transfers between devices with their start and end apart: 18 -> 130, of which waited for: 18 -> 67; matrix products, arithmetic and copies ran while one was open for 6% -> 5% of each run, Pallas kernels for 0% -> 0%
where the time goes in v1:
time: 1470 us
  waiting for transfers between devices  828 us (56%)
  starting transfers between devices  290 us (20%)
  local copies, waits for them, and re-layouts  149 us (10%)
  matrix products  138 us (9%)
  other arithmetic  47.5 us (3%)
    reduce_scatter x8, waiting for transfers between devices, head_step(): lax.psum_scatter(jnp.concatenate([key_grads, value_grads], axis=2), 'leaf...  631 us
    ppermute x56, starting transfers between devices, head_step(): from_right = lax.ppermute(from_right, 'leaf', backward)  271 us
    ppermute x64, waiting for transfers between devices, head_step(): from_left = lax.ppermute(from_left, 'leaf', forward)  177 us
    concatenate x8, local copies, waits for them, and re-layouts, head_step(): jnp.concatenate([key_grads, value_grads], axis=2)  43.4 us
  transfers between devices with their start and end apart: 130, of which 67 were waited for; matrix products, arithmetic and copies ran while one was open for 5% of the time, Pallas kernels for 0%

profile of v1, /device:TPU:1, one launch (start us, length us, event | category | flops | bytes accessed | tf_op | source)
XLA Modules:
  0.0 1471.8 jit_solution(5021965165384656302)
XLA Ops:
  12.9 5.8 all-to-all-start
  24.3 9.5 all-to-all-done
  38.7 1397.0 %while.19 = (s32[]{:T(128)}, bf16[8,4,32,640]{3,2,1,0:T(8,128)(2,1)}, bf16[8,4,32,640]{3,2,1,0:T(8,128)(2,1)}, bf16[8,8,32,256]{3,1,2,0:T(8,128)(2,1)}, bf16[8,4...) while((s32[]{:T(128)}, ...), condition=%wide.region_8.9_spmd.clone, body=%wide.region_1.8_spmd.clone.sunk | while | flops 2550151680 | bytes 146079504 | solution.py:202
  93.2 8.5 collective-permute-done.14
  134.0 75.7 %reduce-scatter.2.cloned.1.call-done = f32[8,32,256]{2,0,1:T(8,128)} async-done(((f32[8,512,256]{2,0,1:T(8,128)}), f32[8,32,256]{2,0,1:T(8,128)}) %reduce-scatter.2.cloned.1.call-update) | async-done | bytes 262160 | tf_op jit(solution)/shard_map/while/body/eval_jaxpr/reduce_scatter | solution.py:190
  257.9 5.5 collective-permute-start.13
  265.9 7.1 collective-permute-done.14
  305.4 79.3 %reduce-scatter.2.cloned.1.call-done = f32[8,32,256]{2,0,1:T(8,128)} async-done(((f32[8,512,256]{2,0,1:T(8,128)}), f32[8,32,256]{2,0,1:T(8,128)}) %reduce-scatter.2.cloned.1.call-update) | async-done | bytes 262160 | tf_op jit(solution)/shard_map/while/body/eval_jaxpr/reduce_scatter | solution.py:190
  440.9 7.1 collective-permute-done.14
  480.4 79.3 %reduce-scatter.2.cloned.1.call-done = f32[8,32,256]{2,0,1:T(8,128)} async-done(((f32[8,512,256]{2,0,1:T(8,128)}), f32[8,32,256]{2,0,1:T(8,128)}) %reduce-scatter.2.cloned.1.call-update) | async-done | bytes 262160 | tf_op jit(solution)/shard_map/while/body/eval_jaxpr/reduce_scatter | solution.py:190
  607.8 5.5 collective-permute-start.13
  615.8 7.1 collective-permute-done.14
  655.2 79.3 %reduce-scatter.2.cloned.1.call-done = f32[8,32,256]{2,0,1:T(8,128)} async-done(((f32[8,512,256]{2,0,1:T(8,128)}), f32[8,32,256]{2,0,1:T(8,128)}) %reduce-scatter.2.cloned.1.call-update) | async-done | bytes 262160 | tf_op jit(solution)/shard_map/while/body/eval_jaxpr/reduce_scatter | solution.py:190
  790.7 7.1 collective-permute-done.14
  830.1 79.3 %reduce-scatter.2.cloned.1.call-done = f32[8,32,256]{2,0,1:T(8,128)} async-done(((f32[8,512,256]{2,0,1:T(8,128)}), f32[8,32,256]{2,0,1:T(8,128)}) %reduce-scatter.2.cloned.1.call-update) | async-done | bytes 262160 | tf_op jit(solution)/shard_map/while/body/eval_jaxpr/reduce_scatter | solution.py:190
  965.6 7.1 collective-permute-done.14
  1005.1 79.2 %reduce-scatter.2.cloned.1.call-done = f32[8,32,256]{2,0,1:T(8,128)} async-done(((f32[8,512,256]{2,0,1:T(8,128)}), f32[8,32,256]{2,0,1:T(8,128)}) %reduce-scatter.2.cloned.1.call-update) | async-done | bytes 262160 | tf_op jit(solution)/shard_map/while/body/eval_jaxpr/reduce_scatter | solution.py:190
  1140.4 7.1 collective-permute-done.14
  1179.9 79.3 %reduce-scatter.2.cloned.1.call-done = f32[8,32,256]{2,0,1:T(8,128)} async-done(((f32[8,512,256]{2,0,1:T(8,128)}), f32[8,32,256]{2,0,1:T(8,128)}) %reduce-scatter.2.cloned.1.call-update) | async-done | bytes 262160 | tf_op jit(solution)/shard_map/while/body/eval_jaxpr/reduce_scatter | solution.py:190
  1307.3 5.5 collective-permute-start.13
  1315.3 7.1 collective-permute-done.14
  1354.8 79.2 %reduce-scatter.2.cloned.1.call-done = f32[8,32,256]{2,0,1:T(8,128)} async-done(((f32[8,512,256]{2,0,1:T(8,128)}), f32[8,32,256]{2,0,1:T(8,128)}) %reduce-scatter.2.cloned.1.call-update) | async-done | bytes 262160 | tf_op jit(solution)/shard_map/while/body/eval_jaxpr/reduce_scatter | solution.py:190
  1440.9 6.7 all-to-all-start.1
  1452.5 10.0 all-to-all-done.1
  (873 shorter events, 715.0 us)
Async XLA Ops:
  12.9 20.9 %all-to-all-start = ((bf16[8,32,2048]{2,1,0:T(8,128)(2,1)}), bf16[8,32,2048]{2,1,0:T(8,128)(2,1)}, u32[]{:S(2)}, u32[]{:S(2)}) async-start(bf16[8,32,2048]{2,1,0:T(8,128)(2,1)} %copy.66), calls=%async_computation.1 | async-start | bytes 2097152 | tf_op jit(solution)/shard_map/all_to_all | solution.py:130
  38.7 171.1 %reduce-scatter.2.cloned.1.call-start = ((), (), s32[]{:S(2)}) async-start(), calls=%async_computation.3 | async-start | bytes 4456448 | tf_op jit(solution)/shard_map/while/body/eval_jaxpr/reduce_scatter | solution.py:190
  39.7 9.9 collective-permute-start
  41.1 8.6 collective-permute-start.1
  93.1 8.5 collective-permute-start.14
  211.4 173.3 %reduce-scatter.2.cloned.1.call-start = ((), (), s32[]{:S(2)}) async-start(), calls=%async_computation.3 | async-start | bytes 4456448 | tf_op jit(solution)/shard_map/while/body/eval_jaxpr/reduce_scatter | solution.py:190
  212.5 8.4 collective-permute-start
  386.3 173.4 %reduce-scatter.2.cloned.1.call-start = ((), (), s32[]{:S(2)}) async-start(), calls=%async_computation.3 | async-start | bytes 4456448 | tf_op jit(solution)/shard_map/while/body/eval_jaxpr/reduce_scatter | solution.py:190
  424.5 8.4 collective-permute-start.10
  424.5 8.4 collective-permute-start.11
  561.3 173.2 %reduce-scatter.2.cloned.1.call-start = ((), (), s32[]{:S(2)}) async-start(), calls=%async_computation.3 | async-start | bytes 4456448 | tf_op jit(solution)/shard_map/while/body/eval_jaxpr/reduce_scatter | solution.py:190
  562.4 8.4 collective-permute-start
  736.1 173.3 %reduce-scatter.2.cloned.1.call-start = ((), (), s32[]{:S(2)}) async-start(), calls=%async_computation.3 | async-start | bytes 4456448 | tf_op jit(solution)/shard_map/while/body/eval_jaxpr/reduce_scatter | solution.py:190
  774.2 8.4 collective-permute-start.10
  774.2 8.4 collective-permute-start.11
  911.0 173.2 %reduce-scatter.2.cloned.1.call-start = ((), (), s32[]{:S(2)}) async-start(), calls=%async_computation.3 | async-start | bytes 4456448 | tf_op jit(solution)/shard_map/while/body/eval_jaxpr/reduce_scatter | solution.py:190
  912.1 8.4 collective-permute-start
  949.2 8.4 collective-permute-start.10
  949.2 8.4 collective-permute-start.11
  1085.9 173.3 %reduce-scatter.2.cloned.1.call-start = ((), (), s32[]{:S(2)}) async-start(), calls=%async_computation.3 | async-start | bytes 4456448 | tf_op jit(solution)/shard_map/while/body/eval_jaxpr/reduce_scatter | solution.py:190
  1124.0 8.4 collective-permute-start.10
  1124.0 8.4 collective-permute-start.11
  1260.8 173.2 %reduce-scatter.2.cloned.1.call-start = ((), (), s32[]{:S(2)}) async-start(), calls=%async_computation.3 | async-start | bytes 4456448 | tf_op jit(solution)/shard_map/while/body/eval_jaxpr/reduce_scatter | solution.py:190
  1440.9 21.7 %all-to-all-start.1 = ((bf16[8,32,2048]{2,1,0:T(8,128)(2,1)}), bf16[8,32,2048]{2,1,0:T(8,128)(2,1)S(1)}, u32[]{:S(2)}, u32[]{:S(2)}) async-start(bf16[8,32,2048]{2,1,0:T(8,128)(2,1)} %copy.74), calls=%async_computation.2 | async-start | bytes 2097152 | tf_op jit(solution)/shard_map/all_to_all | solution.py:220
  (188 other events, 1484.0 us)
Sparse Core Ops, SparseCore 0:
  130.1 79.5 reduce-scatter.1
  301.5 83.1 reduce-scatter.1
  476.5 83.1 reduce-scatter.1
  651.3 83.1 reduce-scatter.1
  826.3 83.1 reduce-scatter.1
  1001.2 82.9 reduce-scatter.1
  1176.0 83.1 reduce-scatter.1
  1350.9 83.0 reduce-scatter.1
